TPU v7x, 256 devices: a whole 4x4x8 slice. The times are simulated.
256 devices in a mesh: chip: 2 (over core), row: 16 (over x, y), grp: 8 (over z).
Axes of the slice: x: 4, y: 4, z: 8, core: 2. Of those that a mesh axis runs over, the one named last changes fastest.
Arguments:
- old_velocity: float32 [2, 4096, 4096], P(None, 'row', ('chip', 'grp')), may hold values from -6 to 6
- surface_stress: float32 [2, 4096, 4096], P(None, 'row', ('chip', 'grp')), may hold values from -6 to 6
- mass_term: float32 [4096, 4096], P('row', ('chip', 'grp')), may hold values from 0.2 to 2
- ocean_drag: float32 [4096, 4096], P('row', ('chip', 'grp')), may hold values from 0.1 to 1
- strength: float32 [4096, 4096], P('row', ('chip', 'grp')), may hold values from 1 to 10
- ice_mask: int32 [4096, 4096], P('row', ('chip', 'grp')), may hold values from 0 to 1, as said below
- ocean_mask: int32 [4096, 4096], P('row', ('chip', 'grp')), may hold values 0 or 1
- ice_blocks: int32 [16, 32], P(('chip', 'grp')), may hold values from 0 to 63, as said below
Outputs:
- new_velocity: float32 [2, 4096, 4096], P(None, 'row', ('chip', 'grp'))
Inputs may be any that keep to these rules, and one draw needn't show every extreme that they name: `ice_blocks`: entry n of row c names block n % 4 (row-major over the blocks of 128 x 128 cells of a tile) of tile row n // 4 in tile column c. Each row lists 32 different blocks; the blocks of one tile stand together, tiles with more listed blocks first; all 4 blocks of the last tile row of every column are listed. The entry at place k of a row is owned by tile row k % 16 of that column, as its block number k // 16. `ice_mask`: ice lies only in cells of the blocks listed in ice_blocks.
All inputs are finite; a program needn't handle non-finite values. No bound on the sum of `ocean_mask` on one device may be relied on, other than what follows from the above.
Results may differ from a plain program's by a relative error of at most 0.00011.
Values sent between devices are 32-bit elements; how exact they have to be, the bound alone decides.
No kernel may reach another device: no remote copies, remote signals or barrier semaphores. Data moves between devices by JAX's collectives and lax.ppermute only.
A program may use at most 128 MiB of HBM per device.

v0:
```python
import jax
import jax.numpy as jnp
from jax import lax
from jax.sharding import PartitionSpec as P

BS = 128
KRYLOV = 2
CYCLES = 2
SWEEPS = 2
RELAX = 0.8
DMIN_SQ = 0.25


def extended(array, sides, width):
    for axis, dim in sides:
        size, length = (lax.axis_size(axis), array.shape[dim])
        up = [(i, (i + 1) % size) for i in range(size - 1)]
        down = [(j, i) for i, j in up]
        last = lax.slice_in_dim(array, length - width, length, axis=dim)
        initial = lax.slice_in_dim(array, 0, width, axis=dim)
        before = lax.ppermute(last, axis, up)
        after = lax.ppermute(initial, axis, down)
        array = jnp.concatenate([before, array, after], axis=dim)
    return array


def stencil(padded, zeta_field, diag_field):

    def pieces(field):
        center = field[..., 1:-1, 1:-1]
        second_x = field[..., 2:, 1:-1] + field[..., :-2, 1:-1] - 2.0 * center
        second_y = field[..., 1:-1, 2:] + field[..., 1:-1, :-2] - 2.0 * center
        mixed = 0.25 * (
            field[..., 2:, 2:] - field[..., 2:, :-2] - field[..., :-2, 2:] + field[..., :-2, :-2]
        )
        return (center, second_x, second_y, mixed)

    part_u = pieces(padded[..., 0, :, :])
    part_v = pieces(padded[..., 1, :, :])
    along_u = (
        diag_field * part_u[0]
        - 1.25 * zeta_field * part_u[1]
        - 0.25 * zeta_field * part_u[2]
        - zeta_field * part_v[3]
    )
    along_v = (
        diag_field * part_v[0]
        - 0.25 * zeta_field * part_v[1]
        - 1.25 * zeta_field * part_v[2]
        - zeta_field * part_u[3]
    )
    return jnp.stack([along_u, along_v], axis=-3)


def precondition(vector, zeta_blocks, diag_blocks):
    diagonal_total = (diag_blocks + 3.0 * zeta_blocks)[:, None]
    iterate = vector / diagonal_total
    for relaxation in range(SWEEPS):
        padded = jnp.pad(iterate, ((0, 0), (0, 0), (1, 1), (1, 1)))
        iterate = (
            iterate + RELAX * (vector - stencil(padded, zeta_blocks, diag_blocks)) / diagonal_total
        )
    return iterate


def least_squares(hessenberg, start_norm):
    steps_count = hessenberg.shape[1]
    row_list = [hessenberg[i] for i in range(steps_count + 1)]
    target_vec = [start_norm] + [jnp.zeros((), jnp.float32) for i in range(steps_count)]
    for j in range(steps_count):
        upper = row_list[j][j]
        lower = row_list[j + 1][j]
        radius = jnp.sqrt(upper * upper + lower * lower)
        cosine = upper / radius
        sine_part = lower / radius
        first_row = cosine * row_list[j] + sine_part * row_list[j + 1]
        second_row = -sine_part * row_list[j] + cosine * row_list[j + 1]
        row_list[j], row_list[j + 1] = (first_row, second_row)
        first_val = cosine * target_vec[j] + sine_part * target_vec[j + 1]
        second_val = -sine_part * target_vec[j] + cosine * target_vec[j + 1]
        target_vec[j], target_vec[j + 1] = (first_val, second_val)
    weights_out = [None] * steps_count
    for j in range(steps_count - 1, -1, -1):
        accum = target_vec[j]
        for i in range(j + 1, steps_count):
            accum = accum - row_list[j][i] * weights_out[i]
        weights_out[j] = accum / row_list[j][j]
    return weights_out


def grid_to_blocks(tile_grid):
    channels, tile_rows, tile_cols = tile_grid.shape
    shaped = tile_grid.reshape(channels, tile_rows // BS, BS, tile_cols // BS, BS).transpose(
        1, 3, 0, 2, 4
    )
    return shaped.reshape(tile_rows // BS * (tile_cols // BS), channels, BS * BS)


def blocks_to_grid(blocks, tile_rows, tile_cols):
    channels = blocks.shape[1]
    shaped = blocks.reshape(tile_rows // BS, tile_cols // BS, channels, BS, BS).transpose(
        2, 0, 3, 1, 4
    )
    return shaped.reshape(channels, tile_rows, tile_cols)


def select(matrix, blocks):
    return jnp.einsum("st,tcx->scx", matrix, blocks, precision=lax.Precision.HIGHEST)


def shards(
    old_velocity, surface_stress, mass_term, ocean_drag, strength, ice_mask, ocean_mask, ice_blocks
):
    tile_rows = old_velocity.shape[1]
    tile_cols = old_velocity.shape[2]
    tile_count = tile_rows // BS * (tile_cols // BS)
    padded = extended(old_velocity, (("row", 1), (("chip", "grp"), 2)), 1)
    flow_u = padded[0]
    flow_v = padded[1]
    strain_xx = 0.5 * (flow_u[2:, 1:-1] - flow_u[:-2, 1:-1])
    strain_yy = 0.5 * (flow_v[1:-1, 2:] - flow_v[1:-1, :-2])
    strain_xy = 0.25 * (flow_u[1:-1, 2:] - flow_u[1:-1, :-2] + flow_v[2:, 1:-1] - flow_v[:-2, 1:-1])
    deform_sq = (
        1.25 * (strain_xx * strain_xx + strain_yy * strain_yy)
        + strain_xy * strain_xy
        + 1.5 * strain_xx * strain_yy
    )
    is_ocean = ocean_mask.astype(jnp.float32)
    zeta_tile = (
        is_ocean * ice_mask.astype(jnp.float32) * strength / (2.0 * jnp.sqrt(deform_sq + DMIN_SQ))
    )
    diag_tile = is_ocean * (mass_term + ocean_drag) + (1.0 - is_ocean)
    rhs_tile = is_ocean * (surface_stress + mass_term * old_velocity)
    coef_blocks = grid_to_blocks(
        jnp.concatenate([zeta_tile[None], diag_tile[None], rhs_tile], axis=0)
    )
    row_count = lax.axis_size("row")
    my_row = lax.axis_index("row")
    listed = ice_blocks[0]
    list_len = listed.shape[0]
    capacity = (tile_count + row_count - 1) // row_count
    slot_count = list_len // row_count
    rank_list = jnp.arange(list_len, dtype=jnp.int32)
    owner_row = rank_list % row_count
    source = listed // tile_count
    inside = listed % tile_count
    earlier = (
        (source[None, :] == source[:, None])
        & (owner_row[None, :] == owner_row[:, None])
        & (rank_list[None, :] < rank_list[:, None])
    )
    position = jnp.sum(earlier.astype(jnp.int32), axis=1)
    target = owner_row * capacity + position
    from_me = (source == my_row).astype(jnp.float32)
    place_ids = jnp.arange(row_count * capacity, dtype=jnp.int32)
    pick_target = (target[:, None] == place_ids[None, :]).astype(jnp.float32) * from_me[:, None]
    pick_inside = (inside[:, None] == jnp.arange(tile_count, dtype=jnp.int32)[None, :]).astype(
        jnp.float32
    )
    send_matrix = jnp.dot(pick_target.T, pick_inside, precision=lax.Precision.HIGHEST)
    owned_ranks = my_row + row_count * jnp.arange(slot_count, dtype=jnp.int32)
    arrival = jnp.take(source * capacity + position, owned_ranks)
    receive_matrix = (arrival[:, None] == place_ids[None, :]).astype(jnp.float32)

    def tile_operator(tile_vector):
        tile_grid = blocks_to_grid(tile_vector, tile_rows, tile_cols)
        grown = extended(tile_grid, (("row", 1), (("chip", "grp"), 2)), 1)
        return grid_to_blocks(stencil(grown, zeta_tile, diag_tile))

    outgoing = select(send_matrix, coef_blocks)
    local_coef = select(
        receive_matrix, lax.all_to_all(outgoing, "row", split_axis=0, concat_axis=0, tiled=True)
    )
    rhs = local_coef[:, 2:4]

    def to_tiles(vector):
        returned = lax.all_to_all(
            select(receive_matrix.T, vector), "row", split_axis=0, concat_axis=0, tiled=True
        )
        return select(send_matrix.T, returned)

    def apply_system(vector):
        images = tile_operator(to_tiles(vector))
        return select(
            receive_matrix,
            lax.all_to_all(
                select(send_matrix, images), "row", split_axis=0, concat_axis=0, tiled=True
            ),
        )

    zeta_blocks = local_coef[:, 0].reshape(-1, BS, BS)
    diag_blocks = local_coef[:, 1].reshape(-1, BS, BS)
    solution = jnp.zeros_like(rhs)
    for restart in range(CYCLES):
        if restart == 0:
            residual = rhs
        else:
            residual = rhs - apply_system(solution)
        start_norm = jnp.sqrt(lax.psum(jnp.sum(residual * residual), ("chip", "row", "grp")))
        basis_list = [residual / start_norm]
        directions = []
        hessenberg = jnp.zeros((KRYLOV + 1, KRYLOV), jnp.float32)
        for arnoldi in range(KRYLOV):
            apply_vector = basis_list[arnoldi]
            shaped = apply_vector.reshape(apply_vector.shape[0], 2, BS, BS)
            direction = precondition(shaped, zeta_blocks, diag_blocks).reshape(apply_vector.shape)
            directions.append(direction)
            images = apply_system(direction)
            local_products = jnp.stack([jnp.sum(images * vector) for vector in basis_list])
            products = lax.psum(local_products, ("chip", "row", "grp"))
            for i in range(arnoldi + 1):
                images = images - products[i] * basis_list[i]
            new_norm = jnp.sqrt(lax.psum(jnp.sum(images * images), ("chip", "row", "grp")))
            hessenberg = (
                hessenberg.at[: arnoldi + 1, arnoldi]
                .set(products)
                .at[arnoldi + 1, arnoldi]
                .set(new_norm)
            )
            if arnoldi + 1 < KRYLOV:
                basis_list.append(images / new_norm)
        weights_out = least_squares(hessenberg, start_norm)
        for arnoldi in range(KRYLOV):
            solution = solution + weights_out[arnoldi] * directions[arnoldi]
    return blocks_to_grid(to_tiles(solution), tile_rows, tile_cols)


def solution(mesh):
    return jax.shard_map(
        shards,
        mesh=mesh,
        in_specs=(
            P(None, "row", ("chip", "grp")),
            P(None, "row", ("chip", "grp")),
            P("row", ("chip", "grp")),
            P("row", ("chip", "grp")),
            P("row", ("chip", "grp")),
            P("row", ("chip", "grp")),
            P("row", ("chip", "grp")),
            P(("chip", "grp"), None),
        ),
        out_specs=P(None, "row", ("chip", "grp")),
        check_vma=False,
    )
```

profile of v0, /device:TPU:32, one launch (start us, length us, event | category | flops | bytes accessed | tf_op | source)
XLA Modules:
  0.0 1476.0 jit_solution(7888579087613427093)
XLA Ops:
  2.1 4.5 collective-permute-start
  30.5 4.7 copy.87
  35.2 6.8 all-to-all-start
  42.6 53.3 %all-to-all-done = f32[16,4,16384]{2,1,0:T(4,128)} async-done(((f32[16,4,16384]{2,1,0:T(4,128)}), f32[16,4,16384]{2,1,0:T(4,128)}, u32[]{:S(2)}, u32[]{:S(2)}) %all-to-all-start) | async-done | bytes 4194336 | tf_op jit(solution)/shard_map/all_to_all | solution.py:172
  95.9 6.0 fusion
  102.8 85.3 %psum.70 = f32[]{:T(128)} all-reduce(f32[]{:T(128)} %multiply_reduce_fusion.11), channel_id=1, replica_groups=mesh['chip'=2,'row'=16,'grp'=8] {'chip','row','grp'}, use_global_device_ids=true, to_apply=%region_2.3 | all-reduce | flops 1 | bytes 8 | tf_op jit(solution)/shard_map/psum | solution.py:199
  194.5 31.6 %all_to_all.60 = f32[16,2,16384]{2,1,0:T(2,128)S(1)} all-to-all(f32[16,2,16384]{2,1,0:T(2,128)S(1)} %copy.89), channel_id=1, replica_groups=mesh['chip'=2,'row'=16,'grp'=8] {'row'}, dimensions={0} | all-to-all | bytes 4194304 | tf_op jit(solution)/shard_map/all_to_all | solution.py:177
  255.4 32.3 %all_to_all.61 = f32[16,2,16384]{2,1,0:T(2,128)S(1)} all-to-all(f32[16,2,16384]{2,1,0:T(2,128)S(1)} %copy.95), channel_id=1, replica_groups=mesh['chip'=2,'row'=16,'grp'=8] {'row'}, dimensions={0} | all-to-all | bytes 4194304 | tf_op jit(solution)/shard_map/all_to_all | solution.py:186
  290.5 75.4 %psum.71 = f32[1]{0:T(128)} all-reduce(f32[1]{0:T(128)} %bitcast.19), channel_id=1, replica_groups=mesh['chip'=2,'row'=16,'grp'=8] {'chip','row','grp'}, use_global_device_ids=true, to_apply=%region_4.5 | all-reduce | flops 1 | bytes 8 | tf_op jit(solution)/shard_map/psum | solution.py:210
  367.4 73.1 %psum.72 = f32[]{:T(128)} all-reduce(f32[]{:T(128)} %get-tuple-element.107), channel_id=1, replica_groups=mesh['chip'=2,'row'=16,'grp'=8] {'chip','row','grp'}, use_global_device_ids=true, to_apply=%region_6.7 | all-reduce | flops 1 | bytes 8 | tf_op jit(solution)/shard_map/psum | solution.py:213
  449.0 32.2 %all_to_all.62 = f32[16,2,16384]{2,1,0:T(2,128)S(1)} all-to-all(f32[16,2,16384]{2,1,0:T(2,128)S(1)} %copy.97), channel_id=1, replica_groups=mesh['chip'=2,'row'=16,'grp'=8] {'row'}, dimensions={0} | all-to-all | bytes 4194304 | tf_op jit(solution)/shard_map/all_to_all | solution.py:177
  489.6 4.5 collective-permute-start.8
  520.5 6.9 all-to-all-start.4
  529.4 26.6 %all-to-all-done.4 = f32[16,2,16384]{2,1,0:T(2,128)} async-done(((f32[16,2,16384]{2,1,0:T(2,128)}), f32[16,2,16384]{2,1,0:T(2,128)}, u32[]{:S(2)}, u32[]{:S(2)}) %all-to-all-start.4) | async-done | bytes 2097184 | tf_op jit(solution)/shard_map/all_to_all | solution.py:186
  561.9 76.9 %psum.73 = f32[2]{0:T(128)S(1)} all-reduce(f32[2]{0:T(128)S(1)} %pad_maximum_fusion.12), channel_id=1, replica_groups=mesh['chip'=2,'row'=16,'grp'=8] {'chip','row','grp'}, use_global_device_ids=true, to_apply=%region_10.11 | all-reduce | flops 2 | bytes 16 | tf_op jit(solution)/shard_map/psum | solution.py:210
  645.1 73.5 %psum.74 = f32[]{:T(128)} all-reduce(f32[]{:T(128)} %multiply_reduce_fusion.6), channel_id=1, replica_groups=mesh['chip'=2,'row'=16,'grp'=8] {'chip','row','grp'}, use_global_device_ids=true, to_apply=%region_12.13 | all-reduce | flops 1 | bytes 8 | tf_op jit(solution)/shard_map/psum | solution.py:213
  732.8 32.3 %all_to_all.63 = f32[16,2,16384]{2,1,0:T(2,128)S(1)} all-to-all(f32[16,2,16384]{2,1,0:T(2,128)S(1)} %copy.105), channel_id=1, replica_groups=mesh['chip'=2,'row'=16,'grp'=8] {'row'}, dimensions={0} | all-to-all | bytes 4194304 | tf_op jit(solution)/shard_map/all_to_all | solution.py:177
  769.9 4.7 collective-permute-start.12
  794.3 33.2 %all_to_all.64 = f32[16,2,16384]{2,1,0:T(2,128)S(1)} all-to-all(f32[16,2,16384]{2,1,0:T(2,128)S(1)} %copy.111), channel_id=1, replica_groups=mesh['chip'=2,'row'=16,'grp'=8] {'row'}, dimensions={0} | all-to-all | bytes 4194304 | tf_op jit(solution)/shard_map/all_to_all | solution.py:186
  830.3 74.5 %psum.75 = f32[]{:T(128)} all-reduce(f32[]{:T(128)} %get-tuple-element.192), channel_id=1, replica_groups=mesh['chip'=2,'row'=16,'grp'=8] {'chip','row','grp'}, use_global_device_ids=true, to_apply=%region_14.15 | all-reduce | flops 1 | bytes 8 | tf_op jit(solution)/shard_map/psum | solution.py:199
  911.2 31.7 %all_to_all.65 = f32[16,2,16384]{2,1,0:T(2,128)S(1)} all-to-all(f32[16,2,16384]{2,1,0:T(2,128)S(1)} %copy.113), channel_id=1, replica_groups=mesh['chip'=2,'row'=16,'grp'=8] {'row'}, dimensions={0} | all-to-all | bytes 4194304 | tf_op jit(solution)/shard_map/all_to_all | solution.py:177
  947.7 4.5 collective-permute-start.16
  972.2 34.3 %all_to_all.66 = f32[16,2,16384]{2,1,0:T(2,128)S(1)} all-to-all(f32[16,2,16384]{2,1,0:T(2,128)S(1)} %copy.119), channel_id=1, replica_groups=mesh['chip'=2,'row'=16,'grp'=8] {'row'}, dimensions={0} | all-to-all | bytes 4194304 | tf_op jit(solution)/shard_map/all_to_all | solution.py:186
  1009.2 73.2 %psum.76 = f32[1]{0:T(128)} all-reduce(f32[1]{0:T(128)} %bitcast.61), channel_id=1, replica_groups=mesh['chip'=2,'row'=16,'grp'=8] {'chip','row','grp'}, use_global_device_ids=true, to_apply=%region_16.17 | all-reduce | flops 1 | bytes 8 | tf_op jit(solution)/shard_map/psum | solution.py:210
  1083.9 73.0 %psum.77 = f32[]{:T(128)} all-reduce(f32[]{:T(128)} %get-tuple-element.105), channel_id=1, replica_groups=mesh['chip'=2,'row'=16,'grp'=8] {'chip','row','grp'}, use_global_device_ids=true, to_apply=%region_18.19 | all-reduce | flops 1 | bytes 8 | tf_op jit(solution)/shard_map/psum | solution.py:213
  1163.3 32.2 %all_to_all.67 = f32[16,2,16384]{2,1,0:T(2,128)S(1)} all-to-all(f32[16,2,16384]{2,1,0:T(2,128)S(1)} %copy.121), channel_id=1, replica_groups=mesh['chip'=2,'row'=16,'grp'=8] {'row'}, dimensions={0} | all-to-all | bytes 4194304 | tf_op jit(solution)/shard_map/all_to_all | solution.py:177
  1200.2 4.5 collective-permute-start.20
  1226.0 6.5 all-to-all-start.10
  1233.2 27.9 %all-to-all-done.10 = f32[16,2,16384]{2,1,0:T(2,128)S(1)} async-done(((f32[16,2,16384]{2,1,0:T(2,128)}), f32[16,2,16384]{2,1,0:T(2,128)S(1)}, u32[]{:S(2)}, u32[]{:S(2)}) %all-to-all-start.10) | async-done | bytes 2097184 | tf_op jit(solution)/shard_map/all_to_all | solution.py:186
  1266.9 76.5 %psum.78 = f32[2]{0:T(128)S(1)} all-reduce(f32[2]{0:T(128)S(1)} %pad_maximum_fusion.13), channel_id=1, replica_groups=mesh['chip'=2,'row'=16,'grp'=8] {'chip','row','grp'}, use_global_device_ids=true, to_apply=%region_21.22 | all-reduce | flops 2 | bytes 16 | tf_op jit(solution)/shard_map/psum | solution.py:210
  1350.6 73.4 %psum.79 = f32[]{:T(128)} all-reduce(f32[]{:T(128)} %multiply_reduce_fusion), channel_id=1, replica_groups=mesh['chip'=2,'row'=16,'grp'=8] {'chip','row','grp'}, use_global_device_ids=true, to_apply=%region_23.24 | all-reduce | flops 1 | bytes 8 | tf_op jit(solution)/shard_map/psum | solution.py:213
  1439.1 32.2 %all_to_all.68 = f32[16,2,16384]{2,1,0:T(2,128)S(1)} all-to-all(f32[16,2,16384]{2,1,0:T(2,128)S(1)} %copy.129), channel_id=1, replica_groups=mesh['chip'=2,'row'=16,'grp'=8] {'row'}, dimensions={0} | all-to-all | bytes 4194304 | tf_op jit(solution)/shard_map/all_to_all | solution.py:177
  (324 shorter events, 245.5 us)
Async XLA Ops:
  0.8 9.7 collective-permute-start.1
  2.1 8.5 collective-permute-start
  10.8 9.7 collective-permute-start.3
  14.5 9.6 collective-permute-start.2
  35.2 60.8 %all-to-all-start = ((f32[16,4,16384]{2,1,0:T(4,128)}), f32[16,4,16384]{2,1,0:T(4,128)}, u32[]{:S(2)}, u32[]{:S(2)}) async-start(f32[16,4,16384]{2,1,0:T(4,128)} %copy.87), calls=%async_computation | async-start | bytes 8388608 | tf_op jit(solution)/shard_map/all_to_all | solution.py:172
  191.7 538.2 %copy-start.3 = (f32[2,2,16384]{2,0,1:T(2,128)}, f32[2,2,16384]{2,0,1:T(2,128)S(1)}, u32[]{:S(2)}) copy-start(f32[2,2,16384]{2,0,1:T(2,128)S(1)} %divide_add_fusion.6) | copy-start | bytes 786436
  229.6 5.9 collective-permute-start.5
  230.9 5.8 collective-permute-start.4
  236.9 8.4 collective-permute-start.7
  240.9 8.6 collective-permute-start.6
  446.2 283.7 %copy-start.5 = (f32[2,2,16384]{2,0,1:T(2,128)}, f32[2,2,16384]{2,0,1:T(2,128)S(1)}, u32[]{:S(2)}) copy-start(f32[2,2,16384]{2,0,1:T(2,128)S(1)} %divide_add_fusion.4) | copy-start | bytes 786436
  488.3 5.9 collective-permute-start.9
  489.6 5.8 collective-permute-start.8
  495.6 8.4 collective-permute-start.11
  498.4 9.8 collective-permute-start.10
  520.5 35.5 %all-to-all-start.4 = ((f32[16,2,16384]{2,1,0:T(2,128)}), f32[16,2,16384]{2,1,0:T(2,128)}, u32[]{:S(2)}, u32[]{:S(2)}) async-start(f32[16,2,16384]{2,1,0:T(2,128)} %copy.103), calls=%async_computation.4 | async-start | bytes 4194304 | tf_op jit(solution)/shard_map/all_to_all | solution.py:186
  768.6 6.0 collective-permute-start.13
  769.9 5.8 collective-permute-start.12
  775.9 8.4 collective-permute-start.15
  778.7 9.8 collective-permute-start.14
  946.4 5.9 collective-permute-start.17
  947.7 5.8 collective-permute-start.16
  953.7 8.4 collective-permute-start.19
  955.7 10.7 collective-permute-start.18
  1198.9 5.9 collective-permute-start.21
  1200.2 5.8 collective-permute-start.20
  1206.3 8.4 collective-permute-start.23
  1209.0 9.8 collective-permute-start.22
  1226.0 35.1 %all-to-all-start.10 = ((f32[16,2,16384]{2,1,0:T(2,128)}), f32[16,2,16384]{2,1,0:T(2,128)S(1)}, u32[]{:S(2)}, u32[]{:S(2)}) async-start(f32[16,2,16384]{2,1,0:T(2,128)} %copy.127), calls=%async_computation.10 | async-start | bytes 4194304 | tf_op jit(solution)/shard_map/all_to_all | solution.py:186
  1232.5 113.5 %copy-start.8 = (f32[2,2,16384]{2,0,1:T(2,128)S(1)}, f32[2,2,16384]{2,0,1:T(2,128)}, u32[]{:S(2)}) copy-start(f32[2,2,16384]{2,0,1:T(2,128)} %copy-done.7) | copy-start | bytes 786436
  1232.5 202.5 %copy-start.4 = (f32[2,2,16384]{2,0,1:T(2,128)S(1)}, f32[2,2,16384]{2,0,1:T(2,128)}, u32[]{:S(2)}) copy-start(f32[2,2,16384]{2,0,1:T(2,128)} %copy-done.3) | copy-start | bytes 786436
  1232.5 202.5 %copy-start.6 = (f32[2,2,16384]{2,0,1:T(2,128)S(1)}, f32[2,2,16384]{2,0,1:T(2,128)}, u32[]{:S(2)}) copy-start(f32[2,2,16384]{2,0,1:T(2,128)} %copy-done.5) | copy-start | bytes 786436
  (14 other events, 312.4 us)
where the time goes:
time: 1490 us; the launch traced here: 1480 us
  blocking collectives  1050 us (70%)
  waiting for transfers between devices  154 us (10%)
  starting transfers between devices  91 us (6%)
  local copies, waits for them, and re-layouts  62.4 us (4%)
  matrix products  61.6 us (4%)
  other arithmetic  38 us (3%)
  between operations  22.1 us (1%)
    psum x4, blocking collectives, shards(): products = lax.psum(local_products, ('chip', 'row', 'grp'))  302 us
    psum x4, blocking collectives, shards(): lax.psum(jnp.sum(images * images), ('chip', 'row', 'grp'))  293 us
    all_to_all x6, blocking collectives, to_tiles(): lax.all_to_all(select(receive_matrix.T, vector), 'row', split_axis=0, con...  192 us
    psum x2, blocking collectives, shards(): lax.psum(jnp.sum(residual * residual), ('chip', 'row', 'grp'))  160 us
    all_to_all x3, blocking collectives, apply_system(): lax.all_to_all(select(send_matrix, images), 'row', split_axis=0, concat_a...  99.7 us
    dot_general x24, matrix products, select(): jnp.einsum('st,tcx->scx', matrix, blocks, precision=lax.Precision.HIGHEST)  61.3 us
    all_to_all x2, waiting for transfers between devices, apply_system(): lax.all_to_all(select(send_matrix, images), 'row', split_axis=0, concat_a...  54.5 us
    all_to_all x1, waiting for transfers between devices, shards(): lax.all_to_all(outgoing, 'row', split_axis=0, concat_axis=0, tiled=True)  53.3 us
  transfers between devices with their start and end apart: 27, of which 20 were waited for; matrix products, arithmetic and copies ran while one was open for 1% of the time, Pallas kernels for 0%

commit v1 on v0

--- a/solution.py
+++ b/solution.py
@@ -207,7 +207,7 @@
             directions.append(direction)
             images = apply_system(direction)
             local_products = jnp.stack([jnp.sum(images * vector) for vector in basis_list])
-            products = lax.psum(local_products, ("chip", "row", "grp"))
+            products = lax.psum(lax.psum(local_products, ("row", "grp")), "chip")
             for i in range(arnoldi + 1):
                 images = images - products[i] * basis_list[i]
             new_norm = jnp.sqrt(lax.psum(jnp.sum(images * images), ("chip", "row", "grp")))

time: 1490 us -> 2580 us (1.73)
  blocking collectives: 1050 us -> 2160 us
  waiting for transfers between devices: 154 us -> 127 us
    psum x4 -> x8, blocking collectives: 302 us -> 1390 us  [shards(): products = lax.psum(lax.psum(local_products, ('row', 'grp')), 'chip')]
    all_to_all x3 -> x4, blocking collectives: 99.7 us -> 134 us  [apply_system(): lax.all_to_all(select(send_matrix, images), 'row', split_axis=0, concat_a...]
    all_to_all x2 -> x1, waiting for transfers between devices: 54.5 us -> 27.4 us  [apply_system(): lax.all_to_all(select(send_matrix, images), 'row', split_axis=0, concat_a...]
  transfers between devices with their start and end apart: 27 -> 26, of which waited for: 20 -> 19; matrix products, arithmetic and copies ran while one was open for 1% -> 0% of each run, Pallas kernels for 0% -> 0%
where the time goes in v1:
time: 2580 us; the launch traced here: 2560 us
  blocking collectives  2160 us (84%)
  waiting for transfers between devices  127 us (5%)
  starting transfers between devices  84.2 us (3%)
  local copies, waits for them, and re-layouts  69 us (3%)
  matrix products  61.6 us (2%)
  other arithmetic  37.7 us (1%)
    psum x8, blocking collectives, shards(): products = lax.psum(lax.psum(local_products, ('row', 'grp')), 'chip')  1390 us
    psum x4, blocking collectives, shards(): lax.psum(jnp.sum(images * images), ('chip', 'row', 'grp'))  296 us
    all_to_all x6, blocking collectives, to_tiles(): lax.all_to_all(select(receive_matrix.T, vector), 'row', split_axis=0, con...  188 us
    psum x2, blocking collectives, shards(): lax.psum(jnp.sum(residual * residual), ('chip', 'row', 'grp'))  159 us
    all_to_all x4, blocking collectives, apply_system(): lax.all_to_all(select(send_matrix, images), 'row', split_axis=0, concat_a...  134 us
    dot_general x24, matrix products, select(): jnp.einsum('st,tcx->scx', matrix, blocks, precision=lax.Precision.HIGHEST)  61.4 us
    all_to_all x1, waiting for transfers between devices, shards(): lax.all_to_all(outgoing, 'row', split_axis=0, concat_axis=0, tiled=True)  53.3 us
  transfers between devices with their start and end apart: 26, of which 19 were waited for; matrix products, arithmetic and copies ran while one was open for 0% of the time, Pallas kernels for 0%

profile of v1, /device:TPU:32, one launch (start us, length us, event | category | flops | bytes accessed | tf_op | source)
XLA Modules:
  0.0 2565.0 jit_solution(5857317347306588971)
XLA Ops:
  2.1 4.5 collective-permute-start
  30.5 4.7 copy.87
  35.1 6.8 all-to-all-start
  42.6 53.3 %all-to-all-done = f32[16,4,16384]{2,1,0:T(4,128)} async-done(((f32[16,4,16384]{2,1,0:T(4,128)}), f32[16,4,16384]{2,1,0:T(4,128)}, u32[]{:S(2)}, u32[]{:S(2)}) %all-to-all-start) | async-done | bytes 4194336 | tf_op jit(solution)/shard_map/all_to_all | solution.py:172
  95.9 6.0 fusion
  102.8 85.3 %psum.98 = f32[]{:T(128)} all-reduce(f32[]{:T(128)} %multiply_reduce_fusion.11), channel_id=1, replica_groups=mesh['chip'=2,'row'=16,'grp'=8] {'chip','row','grp'}, use_global_device_ids=true, to_apply=%region_2.3 | all-reduce | flops 1 | bytes 8 | tf_op jit(solution)/shard_map/psum | solution.py:199
  194.5 31.6 %all_to_all.60 = f32[16,2,16384]{2,1,0:T(2,128)S(1)} all-to-all(f32[16,2,16384]{2,1,0:T(2,128)S(1)} %copy.89), channel_id=1, replica_groups=mesh['chip'=2,'row'=16,'grp'=8] {'row'}, dimensions={0} | all-to-all | bytes 4194304 | tf_op jit(solution)/shard_map/all_to_all | solution.py:177
  230.9 4.5 collective-permute-start.4
  255.3 32.3 %all_to_all.61 = f32[16,2,16384]{2,1,0:T(2,128)S(1)} all-to-all(f32[16,2,16384]{2,1,0:T(2,128)S(1)} %copy.95), channel_id=1, replica_groups=mesh['chip'=2,'row'=16,'grp'=8] {'row'}, dimensions={0} | all-to-all | bytes 4194304 | tf_op jit(solution)/shard_map/all_to_all | solution.py:186
  290.4 345.7 %psum.99 = f32[1]{0:T(128)} all-reduce(f32[1]{0:T(128)} %bitcast.19), channel_id=1, replica_groups=mesh['chip'=2,'row'=16,'grp'=8] {'row','grp'}, use_global_device_ids=true, to_apply=%region_4.5 | all-reduce | flops 1 | bytes 8 | tf_op jit(solution)/shard_map/psum | solution.py:210
  640.9 73.3 %psum.101 = f32[]{:T(128)} all-reduce(f32[]{:T(128)} %get-tuple-element.107), channel_id=1, replica_groups=mesh['chip'=2,'row'=16,'grp'=8] {'chip','row','grp'}, use_global_device_ids=true, to_apply=%region_7.8 | all-reduce | flops 1 | bytes 8 | tf_op jit(solution)/shard_map/psum | solution.py:213
  722.7 31.2 %all_to_all.62 = f32[16,2,16384]{2,1,0:T(2,128)S(1)} all-to-all(f32[16,2,16384]{2,1,0:T(2,128)S(1)} %copy.97), channel_id=1, replica_groups=mesh['chip'=2,'row'=16,'grp'=8] {'row'}, dimensions={0} | all-to-all | bytes 4194304 | tf_op jit(solution)/shard_map/all_to_all | solution.py:177
  762.4 4.5 collective-permute-start.8
  793.3 6.6 all-to-all-start.4
  801.1 27.4 %all-to-all-done.4 = f32[16,2,16384]{2,1,0:T(2,128)} async-done(((f32[16,2,16384]{2,1,0:T(2,128)}), f32[16,2,16384]{2,1,0:T(2,128)}, u32[]{:S(2)}, u32[]{:S(2)}) %all-to-all-start.4) | async-done | bytes 2097184 | tf_op jit(solution)/shard_map/all_to_all | solution.py:186
  834.9 343.9 %psum.102 = f32[2]{0:T(128)S(1)} all-reduce(f32[2]{0:T(128)S(1)} %pad_maximum_fusion.12), channel_id=1, replica_groups=mesh['chip'=2,'row'=16,'grp'=8] {'row','grp'}, use_global_device_ids=true, to_apply=%region_11.12 | all-reduce | flops 2 | bytes 16 | tf_op jit(solution)/shard_map/psum | solution.py:210
  1187.4 73.6 %psum.104 = f32[]{:T(128)} all-reduce(f32[]{:T(128)} %multiply_reduce_fusion.6), channel_id=1, replica_groups=mesh['chip'=2,'row'=16,'grp'=8] {'chip','row','grp'}, use_global_device_ids=true, to_apply=%region_14.15 | all-reduce | flops 1 | bytes 8 | tf_op jit(solution)/shard_map/psum | solution.py:213
  1274.4 31.1 %all_to_all.63 = f32[16,2,16384]{2,1,0:T(2,128)S(1)} all-to-all(f32[16,2,16384]{2,1,0:T(2,128)S(1)} %copy.105), channel_id=1, replica_groups=mesh['chip'=2,'row'=16,'grp'=8] {'row'}, dimensions={0} | all-to-all | bytes 4194304 | tf_op jit(solution)/shard_map/all_to_all | solution.py:177
  1310.2 4.5 collective-permute-start.12
  1334.7 33.4 %all_to_all.64 = f32[16,2,16384]{2,1,0:T(2,128)S(1)} all-to-all(f32[16,2,16384]{2,1,0:T(2,128)S(1)} %copy.111), channel_id=1, replica_groups=mesh['chip'=2,'row'=16,'grp'=8] {'row'}, dimensions={0} | all-to-all | bytes 4194304 | tf_op jit(solution)/shard_map/all_to_all | solution.py:186
  1370.9 74.0 %psum.105 = f32[]{:T(128)} all-reduce(f32[]{:T(128)} %get-tuple-element.192), channel_id=1, replica_groups=mesh['chip'=2,'row'=16,'grp'=8] {'chip','row','grp'}, use_global_device_ids=true, to_apply=%region_16.17 | all-reduce | flops 1 | bytes 8 | tf_op jit(solution)/shard_map/psum | solution.py:199
  1451.2 31.7 %all_to_all.65 = f32[16,2,16384]{2,1,0:T(2,128)S(1)} all-to-all(f32[16,2,16384]{2,1,0:T(2,128)S(1)} %copy.113), channel_id=1, replica_groups=mesh['chip'=2,'row'=16,'grp'=8] {'row'}, dimensions={0} | all-to-all | bytes 4194304 | tf_op jit(solution)/shard_map/all_to_all | solution.py:177
  1491.4 4.5 collective-permute-start.16
  1517.7 34.3 %all_to_all.66 = f32[16,2,16384]{2,1,0:T(2,128)S(1)} all-to-all(f32[16,2,16384]{2,1,0:T(2,128)S(1)} %copy.119), channel_id=1, replica_groups=mesh['chip'=2,'row'=16,'grp'=8] {'row'}, dimensions={0} | all-to-all | bytes 4194304 | tf_op jit(solution)/shard_map/all_to_all | solution.py:186
  1554.7 343.6 %psum.106 = f32[1]{0:T(128)} all-reduce(f32[1]{0:T(128)} %bitcast.61), channel_id=1, replica_groups=mesh['chip'=2,'row'=16,'grp'=8] {'row','grp'}, use_global_device_ids=true, to_apply=%region_18.19 | all-reduce | flops 1 | bytes 8 | tf_op jit(solution)/shard_map/psum | solution.py:210
  1903.0 74.6 %psum.108 = f32[]{:T(128)} all-reduce(f32[]{:T(128)} %get-tuple-element.105), channel_id=1, replica_groups=mesh['chip'=2,'row'=16,'grp'=8] {'chip','row','grp'}, use_global_device_ids=true, to_apply=%region_21.22 | all-reduce | flops 1 | bytes 8 | tf_op jit(solution)/shard_map/psum | solution.py:213
  1984.7 31.1 %all_to_all.67 = f32[16,2,16384]{2,1,0:T(2,128)S(1)} all-to-all(f32[16,2,16384]{2,1,0:T(2,128)S(1)} %copy.121), channel_id=1, replica_groups=mesh['chip'=2,'row'=16,'grp'=8] {'row'}, dimensions={0} | all-to-all | bytes 4194304 | tf_op jit(solution)/shard_map/all_to_all | solution.py:177
  2024.2 4.5 collective-permute-start.20
  2050.3 34.0 %all_to_all.68 = f32[16,2,16384]{2,1,0:T(2,128)S(1)} all-to-all(f32[16,2,16384]{2,1,0:T(2,128)S(1)} %copy.127), channel_id=1, replica_groups=mesh['chip'=2,'row'=16,'grp'=8] {'row'}, dimensions={0} | all-to-all | bytes 4194304 | tf_op jit(solution)/shard_map/all_to_all | solution.py:186
  2089.1 343.0 %psum.109 = f32[2]{0:T(128)S(1)} all-reduce(f32[2]{0:T(128)S(1)} %pad_maximum_fusion.13), channel_id=1, replica_groups=mesh['chip'=2,'row'=16,'grp'=8] {'row','grp'}, use_global_device_ids=true, to_apply=%region_24.25 | all-reduce | flops 2 | bytes 16 | tf_op jit(solution)/shard_map/psum | solution.py:210
  2441.0 74.5 %psum.111 = f32[]{:T(128)} all-reduce(f32[]{:T(128)} %multiply_reduce_fusion), channel_id=1, replica_groups=mesh['chip'=2,'row'=16,'grp'=8] {'chip','row','grp'}, use_global_device_ids=true, to_apply=%region_27.28 | all-reduce | flops 1 | bytes 8 | tf_op jit(solution)/shard_map/psum | solution.py:213
  2529.2 31.1 %all_to_all.69 = f32[16,2,16384]{2,1,0:T(2,128)S(1)} all-to-all(f32[16,2,16384]{2,1,0:T(2,128)S(1)} %copy.129), channel_id=1, replica_groups=mesh['chip'=2,'row'=16,'grp'=8] {'row'}, dimensions={0} | all-to-all | bytes 4194304 | tf_op jit(solution)/shard_map/all_to_all | solution.py:177
  (307 shorter events, 258.7 us)
Async XLA Ops:
  0.0 10.6 copy-start
  0.0 10.5 copy-start.8
  0.8 9.7 collective-permute-start.1
  2.1 8.5 collective-permute-start
  10.8 9.7 collective-permute-start.3
  14.5 9.6 collective-permute-start.2
  17.2 7.5 copy-start.1
  17.2 7.5 copy-start.2
  17.2 7.4 copy-start.5
  17.2 7.4 copy-start.6
  35.1 60.8 %all-to-all-start = ((f32[16,4,16384]{2,1,0:T(4,128)}), f32[16,4,16384]{2,1,0:T(4,128)}, u32[]{:S(2)}, u32[]{:S(2)}) async-start(f32[16,4,16384]{2,1,0:T(4,128)} %copy.87), calls=%async_computation | async-start | bytes 8388608 | tf_op jit(solution)/shard_map/all_to_all | solution.py:172
  229.6 5.9 collective-permute-start.5
  230.9 5.8 collective-permute-start.4
  236.9 8.4 collective-permute-start.7
  240.9 8.6 collective-permute-start.6
  761.1 5.9 collective-permute-start.9
  762.4 5.8 collective-permute-start.8
  768.4 8.4 collective-permute-start.11
  771.1 9.9 collective-permute-start.10
  793.3 35.2 %all-to-all-start.4 = ((f32[16,2,16384]{2,1,0:T(2,128)}), f32[16,2,16384]{2,1,0:T(2,128)}, u32[]{:S(2)}, u32[]{:S(2)}) async-start(f32[16,2,16384]{2,1,0:T(2,128)} %copy.103), calls=%async_computation.4 | async-start | bytes 4194304 | tf_op jit(solution)/shard_map/all_to_all | solution.py:186
  1308.9 5.9 collective-permute-start.13
  1310.2 5.8 collective-permute-start.12
  1316.3 8.4 collective-permute-start.15
  1318.7 10.2 collective-permute-start.14
  1490.1 5.9 collective-permute-start.17
  1491.4 5.8 collective-permute-start.16
  1497.4 8.4 collective-permute-start.19
  1499.3 10.7 collective-permute-start.18
  2022.9 5.9 collective-permute-start.21
  2024.2 5.8 collective-permute-start.20
  2030.2 8.4 collective-permute-start.23
  2032.1 10.7 collective-permute-start.22
  (3 other events, 9.8 us)
